TPU v7x, 32 devices: a whole 2x2x4 slice. The times are simulated.
32 devices in a mesh: groups: 2 (over y), col: 4 (over z), aux: 2 (over x), rep: 2 (over core).
Axes of the slice: x: 2, y: 2, z: 4, core: 2. Of those that a mesh axis runs over, the one named last changes fastest.
Arguments:
- b_aux: bfloat16 [4, 4096, 2400], P(('groups', 'aux'), ('col', 'rep')), parts along dimension 0, may hold values from -0.59765625 to 0.59765625
- occ_energies: float32 [2], P('groups'), parts along dimension 0, may hold values from -2 to -0.3
- vir_energies: float32 [4800], P('groups'), parts along dimension 0, may hold values from 0.2 to 3
- owners: int32 [2], replicated, may hold values from 0 to 7
Outputs:
- gamma: float32 [4, 4096, 2400], P(('groups', 'aux'), None, ('col', 'rep')), parts along dimension 0
There are 2 independent parts, one for each index of `groups`. A program takes and returns all parts, laid end to end along the dimension named above; an argument that names none is the same for every part. Nothing has to cross between parts.
Inputs may be any that keep to these rules, and one draw needn't show every extreme that they name: owners[s] is a column shard index in the order of col+rep; owners may repeat.
All inputs are finite; a program needn't handle non-finite values.
Results may differ from a plain program's by a relative error of at most 0.003.
Values may be sent and summed in bfloat16 or wider, within the bound.
No kernel may reach another device: no remote copies, remote signals or barrier semaphores. Data moves between devices by JAX's collectives and lax.ppermute only.
A program may use at most 64 MiB of HBM per device.

v0:
```python
import jax
import jax.numpy as jnp
from jax import lax
from jax.sharding import PartitionSpec as P

os_scale = 1.3


def from_root(value, axis, source):
    kept = jnp.where(lax.axis_index(axis) == source, value, 0).astype(value.dtype)
    return lax.psum(kept, axis)


def column_energy(first, occ_energies, vir_energies, width):
    nvirt = vir_energies.shape[0]
    occ_value = lax.dynamic_index_in_dim(occ_energies, first // nvirt, 0, keepdims=False)
    vir_values = lax.dynamic_slice_in_dim(vir_energies, first % nvirt, width, 0)
    return vir_values - occ_value


def body(b_aux, occ_energies, vir_energies, owners):
    moved = lax.all_to_all(b_aux, ("col", "rep"), split_axis=2, concat_axis=1, tiled=True)
    local_cols = moved[0]
    width = local_cols.shape[1]
    shard_index = lax.axis_index(("col", "rep"))
    energy_mine = column_energy(shard_index * width, occ_energies, vir_energies, width)
    gamma_acc = jnp.zeros(local_cols.shape, jnp.float32)
    for step_index in range(owners.shape[0]):
        owner_shard = owners[step_index]
        owner_cols = from_root(local_cols, ("col", "rep"), owner_shard)
        owner_energy = column_energy(owner_shard * width, occ_energies, vir_energies, width)
        denominator = energy_mine[:, None] + owner_energy[None, :]
        partial_value = lax.dot_general(
            local_cols, owner_cols, (((0,), (0,)), ((), ())), preferred_element_type=jnp.float32
        )
        coupling = lax.psum(partial_value, "aux")
        amplitude = (os_scale * coupling / denominator).astype(jnp.bfloat16)
        gamma_acc = gamma_acc + lax.dot_general(
            owner_cols, amplitude, (((1,), (1,)), ((), ())), preferred_element_type=jnp.float32
        )
    return gamma_acc[None]


def solution(mesh):
    placed = (P(("groups", "aux"), ("col", "rep"), None), P("groups"), P("groups"), P())
    return jax.shard_map(
        body,
        mesh=mesh,
        in_specs=placed,
        out_specs=P(("groups", "aux"), None, ("col", "rep")),
        check_vma=False,
    )
```

profile of v0, /device:TPU:0, one launch (start us, length us, event | category | flops | bytes accessed | tf_op | source)
XLA Modules:
  0.0 311.1 jit_solution(7487857900732730221)
XLA Ops:
  6.5 13.4 %copy.16 = bf16[1,512,2400]{1,0,2:T(2,128)(2,1)} copy(bf16[1,512,2400]{1,2,0:T(8,128)(2,1)} %param.4) | data formatting | bytes 4915200 | tf_op args[0]
  20.0 0.6 broadcast.16
  20.6 16.3 %reduce.2 = bf16[2400,512]{1,0:T(8,128)(2,1)S(1)} reduce(bf16[2400,1,512]{2,1,0:T(2,128)(2,1)} %bitcast.32, bf16[]{:T(256)} %broadcast.16), dimensions={1}, to_apply=%bitcast.30.reduce_sub_computation | reduce | bytes 4915202
  36.9 2.4 reshape.5
  39.3 6.5 %all-to-all-start = ((bf16[8,2,76800]{2,1,0:T(2,128)(2,1)}), bf16[8,2,76800]{2,1,0:T(2,128)(2,1)S(1)}, u32[]{:S(2)}, u32[]{:S(2)}) async-start(bf16[8,2,76800]{2,1,0:T(2,128)(2,1)} %reshape.5), calls=%async_computation | async-start | bytes 4915200 | tf_op jit(solution)/shard_map/all_to_all | solution.py:22
  45.7 0.0 all-reduce.7.cloned.1.call-start
  45.8 0.6 fusion.10
  47.7 54.8 %all-to-all-done = bf16[8,2,76800]{2,1,0:T(2,128)(2,1)S(1)} async-done(((bf16[8,2,76800]{2,1,0:T(2,128)(2,1)}), bf16[8,2,76800]{2,1,0:T(2,128)(2,1)S(1)}, u32[]{:S(2)}, u32[]{:S(2)}) %all-to-all-start) | async-done | bytes 2457632 | tf_op jit(solution)/shard_map/all_to_all | solution.py:22
  102.5 4.4 %reshape.6 = bf16[2400,1,512]{2,1,0:T(2,128)(2,1)} reshape(bf16[8,2,76800]{2,1,0:T(2,128)(2,1)S(1)} %all-to-all-done) | data formatting | bytes 4915200
  107.0 17.2 %bitcast_reduce_fusion = bf16[512,2400]{0,1:T(8,128)(2,1)} fusion(bf16[2400,1,512]{2,1,0:T(2,128)(2,1)} %reshape.6), kind=kLoop, calls=%fused_computation.22 | loop fusion | bytes 4915200 | tf_op jit(solution)/shard_map/all_to_all | solution.py:22
  124.1 2.6 all_to_all.12
  126.8 1.4 copy.15
  128.1 0.2 pad
  128.3 1.1 copy.12
  129.4 2.6 broadcast_select_fusion
  132.1 0.2 all-reduce.5.cloned.1.call-start
  132.3 110.6 %all-reduce.7.cloned.1.call-done = (bf16[4096,300]{0,1:T(8,128)(2,1)}, bf16[4096,300]{0,1:T(8,128)(2,1)}) async-done(((bf16[4096,300]{0,1:T(8,128)(2,1)}, bf16[4096,300]{0,1:T(8,128)(2,1)}), (bf16[4096,300]{0,1:T(8,128)(2,1)}, bf16[4096,300]{0,1:T(8,128)(2,1)})) %all-reduce.7.cloned.1.call-update) | async-done | bytes 4915216 | tf_op jit(solution)/shard_map/psum | solution.py:11
  242.9 4.1 %convolution_bitcast_fusion.1 = f32[300,300]{0,1:T(8,128)} fusion(bf16[4096,300]{0,1:T(8,128)(2,1)} %get-tuple-element.7, bf16[4096,300]{0,1:T(8,128)(2,1)S(1)} %bitcast.34), kind=kOutput, calls=%fused_computation.6 | convolution fusion | flops 737280000 | bytes 5275200 | tf_op jit(solution)/shard_map/dot_general | solution.py:33
  247.0 2.3 convolution_bitcast_fusion
  251.2 0.1 dynamic-slice_subtract_fusion
  251.3 35.9 %all-reduce.5.cloned.1.call-done = (f32[300,300]{0,1:T(8,128)}, f32[300,300]{0,1:T(8,128)}) async-done(((f32[300,300]{0,1:T(8,128)}, f32[300,300]{0,1:T(8,128)}), (f32[300,300]{0,1:T(8,128)}, f32[300,300]{0,1:T(8,128)})) %all-reduce.5.cloned.1.call-update) | async-done | bytes 720016 | tf_op jit(solution)/shard_map/psum | solution.py:36
  287.2 3.5 %fusion.1 = f32[4096,300]{0,1:T(8,128)S(1)} fusion(bf16[4096,300]{0,1:T(8,128)(2,1)} %get-tuple-element.7, f32[300,300]{0,1:T(8,128)} %get-tuple-element.5, f32[300]{0:T(512)S(1)} %get-tuple-element.13, f32[300]{0:T(512)S(1)} %get-tuple-element.12), kind=kOutput, calls=%fused_computation.9 | convolution fusion | flops 737640000 | bytes 7735200 | tf_op jit(solution)/shard_map/dot_general | solution.py:38
  290.7 3.9 %fusion = f32[1,4096,300]{1,2,0:T(8,128)} fusion(f32[4096,300]{0,1:T(8,128)S(1)} %fusion.1, bf16[4096,300]{0,1:T(8,128)(2,1)S(1)} %copy-done.1, f32[300,300]{0,1:T(8,128)S(1)} %copy-done.2, f32[300]{0:T(512)S(1)} %get-tuple-element.11, f32[300]{0:T(512)S(1)} %get-tuple-element.12), kind=kOutput, calls=%fused_computation.1 | convolution fusion | flops 738868800 | bytes 12650400 | tf_op jit(solution)/shard_map/dot_general | solution.py:38
  294.6 9.7 %copy.10 = f32[1,4096,300]{1,0,2:T(1,128)} copy(f32[1,4096,300]{1,2,0:T(8,128)} %fusion) | data formatting | bytes 9830400 | tf_op jit(solution)/shard_map/broadcast_in_dim | solution.py:41
  (12 shorter events, 0.1 us)
Async XLA Ops:
  39.3 6.5 %copy-start.4 = (s32[2]{0:T(128)S(1)}, s32[2]{0:T(128)}, u32[]{:S(2)}) copy-start(s32[2]{0:T(128)} %param.7) | copy-start | bytes 28
  39.3 63.2 %all-to-all-start = ((bf16[8,2,76800]{2,1,0:T(2,128)(2,1)}), bf16[8,2,76800]{2,1,0:T(2,128)(2,1)S(1)}, u32[]{:S(2)}, u32[]{:S(2)}) async-start(bf16[8,2,76800]{2,1,0:T(2,128)(2,1)} %reshape.5), calls=%async_computation | async-start | bytes 4915200 | tf_op jit(solution)/shard_map/all_to_all | solution.py:22
  45.7 197.1 %all-reduce.7.cloned.1.call-start = ((), (), s32[]{:S(2)}) async-start(), calls=%async_computation.2 | async-start | bytes 9961472 | tf_op jit(solution)/shard_map/psum | solution.py:11
  132.1 155.1 %all-reduce.5.cloned.1.call-start = ((), (), s32[]{:S(2)}) async-start(), calls=%async_computation.1 | async-start | bytes 1867776 | tf_op jit(solution)/shard_map/psum | solution.py:36
  242.9 4.1 %copy-start = (bf16[4096,300]{0,1:T(8,128)(2,1)S(1)}, bf16[4096,300]{0,1:T(8,128)(2,1)}, u32[]{:S(2)}) copy-start(bf16[4096,300]{0,1:T(8,128)(2,1)} %get-tuple-element.8) | copy-start | bytes 7372804
  247.0 4.2 %copy-start.3 = (f32[2400]{0:T(1024)S(1)}, f32[2400]{0:T(1024)}, u32[]{:S(2)}) copy-start(f32[2400]{0:T(1024)} %param.6) | copy-start | bytes 28804
  287.2 3.5 %copy-start.1 = (bf16[4096,300]{0,1:T(8,128)(2,1)S(1)}, bf16[4096,300]{0,1:T(8,128)(2,1)}, u32[]{:S(2)}) copy-start(bf16[4096,300]{0,1:T(8,128)(2,1)} %get-tuple-element.8) | copy-start | bytes 7372804
  287.2 3.5 %copy-start.2 = (f32[300,300]{0,1:T(8,128)S(1)}, f32[300,300]{0,1:T(8,128)}, u32[]{:S(2)}) copy-start(f32[300,300]{0,1:T(8,128)} %get-tuple-element.6) | copy-start | bytes 1080004
Sparse Core Ops, SparseCore 0:
  132.2 110.6 all-reduce.6
  249.4 37.7 all-reduce.4
where the time goes:
time: 312 us; the launch traced here: 311 us
  waiting for transfers between devices  201 us (64%)
  local copies, waits for them, and re-layouts  53.6 us (17%)
  other arithmetic  19.1 us (6%)
  between operations  16.7 us (5%)
  matrix products  13.7 us (4%)
  starting transfers between devices  6.72 us (2%)
    psum x1, waiting for transfers between devices, from_root(): return lax.psum(kept, axis)  111 us
    all_to_all x1, waiting for transfers between devices, body(): lax.all_to_all(b_aux, ('col', 'rep'), split_axis=2, concat_axis=1, tiled=...  54.8 us
    psum x1, waiting for transfers between devices, body(): coupling = lax.psum(partial_value, 'aux')  35.9 us
    unnamed x16, local copies, waits for them, and re-layouts  22.1 us
    all_to_all x3, local copies, waits for them, and re-layouts, body(): lax.all_to_all(b_aux, ('col', 'rep'), split_axis=2, concat_axis=1, tiled=...  21.1 us
    unnamed x1, other arithmetic  16.3 us
    broadcast_in_dim x1, local copies, waits for them, and re-layouts, body(): return gamma_acc[None]  9.71 us
    dot_general x2, matrix products, body(): lax.dot_general(owner_cols, amplitude, (((1,), (1,)), ((), ())), preferre...  7.4 us
  transfers between devices with their start and end apart: 3, of which 3 were waited for; matrix products, arithmetic and copies ran while one was open for 0% of the time, Pallas kernels for 0%

commit v1 on v0

--- a/solution.py
+++ b/solution.py
@@ -1,9 +1,35 @@
+import functools
 import jax
 import jax.numpy as jnp
 from jax import lax
 from jax.sharding import PartitionSpec as P
 
 os_scale = 1.3
+
+
+def start_sector(x_in, peer_axis):
+    heard = jax.lax.axis_size(peer_axis)
+    view_out = jax.lax.axis_index(peer_axis)
+    w1, newest = (heard, view_out)
+    before = x_in.shape[2] // w1
+    val = list(x_in.shape)
+    val[2] = before
+    seen_now = val[1]
+    val[1] = seen_now * w1
+    u_next = jnp.zeros(val, x_in.dtype)
+    for q in range(w1):
+        current_block = lax.dynamic_slice_in_dim(x_in, (newest ^ q) * before, before, axis=2)
+        if q:
+            current_block = jax.lax.ppermute(
+                current_block, peer_axis, [(i, i ^ q) for i in range(w1)]
+            )
+        u_next = lax.dynamic_update_slice_in_dim(
+            u_next, current_block, (newest ^ q) * seen_now, axis=1
+        )
+    return u_next
+
+
+process_the_frames = functools.partial(start_sector, peer_axis=("col", "rep"))
 
 
 def from_root(value, axis, source):
@@ -19,7 +45,7 @@
 
 
 def body(b_aux, occ_energies, vir_energies, owners):
-    moved = lax.all_to_all(b_aux, ("col", "rep"), split_axis=2, concat_axis=1, tiled=True)
+    moved = process_the_frames(b_aux)
     local_cols = moved[0]
     width = local_cols.shape[1]
     shard_index = lax.axis_index(("col", "rep"))

time: 312 us -> 253 us (0.81)
  local copies, waits for them, and re-layouts: 53.6 us -> 19.7 us
  other arithmetic: 19.1 us -> 2.72 us
  waiting for transfers between devices: 201 us -> 190 us
  starting transfers between devices: 6.72 us -> 10.4 us
    all_to_all x1 -> x0, waiting for transfers between devices: 54.8 us -> none  [body(): lax.all_to_all(b_aux, ('col', 'rep'), split_axis=2, concat_axis=1, tiled=...]
    ppermute x0 -> x7, waiting for transfers between devices: none -> 28 us  [start_sector(): jax.lax.ppermute(current_block, peer_axis, [(i, i ^ q) for i in range(w1)])]
    unnamed x16 -> x10, local copies, waits for them, and re-layouts: 22.1 us -> 0.02 us
    all_to_all x3 -> x0, local copies, waits for them, and re-layouts: 21.1 us -> none  [body(): lax.all_to_all(b_aux, ('col', 'rep'), split_axis=2, concat_axis=1, tiled=...]
    unnamed x1 -> x0, other arithmetic: 16.3 us -> none
    psum x1, waiting for transfers between devices: 111 us -> 126 us  [from_root(): return lax.psum(kept, axis)]
    ppermute x0 -> x7, starting transfers between devices: none -> 10.2 us  [start_sector(): jax.lax.ppermute(current_block, peer_axis, [(i, i ^ q) for i in range(w1)])]
    all_to_all x1 -> x0, starting transfers between devices: 6.46 us -> none  [body(): lax.all_to_all(b_aux, ('col', 'rep'), split_axis=2, concat_axis=1, tiled=...]
  transfers between devices with their start and end apart: 3 -> 9, of which waited for: 3 -> 6; matrix products, arithmetic and copies ran while one was open for 0% -> 3% of each run, Pallas kernels for 0% -> 0%
where the time goes in v1:
time: 253 us
  waiting for transfers between devices  190 us (75%)
  local copies, waits for them, and re-layouts  19.7 us (8%)
  between operations  16.6 us (7%)
  matrix products  13.6 us (5%)
  starting transfers between devices  10.4 us (4%)
  other arithmetic  2.72 us (1%)
    psum x1, waiting for transfers between devices, from_root(): return lax.psum(kept, axis)  126 us
    psum x1, waiting for transfers between devices, body(): coupling = lax.psum(partial_value, 'aux')  35.9 us
    ppermute x7, waiting for transfers between devices, start_sector(): jax.lax.ppermute(current_block, peer_axis, [(i, i ^ q) for i in range(w1)])  28 us
    ppermute x7, starting transfers between devices, start_sector(): jax.lax.ppermute(current_block, peer_axis, [(i, i ^ q) for i in range(w1)])  10.2 us
    broadcast_in_dim x1, local copies, waits for them, and re-layouts, body(): return gamma_acc[None]  9.71 us
    dot_general x2, matrix products, body(): lax.dot_general(owner_cols, amplitude, (((1,), (1,)), ((), ())), preferre...  7.23 us
    dot_general x2, matrix products, body(): lax.dot_general(local_cols, owner_cols, (((0,), (0,)), ((), ())), preferr...  6.33 us
    dynamic_update_slice x8, local copies, waits for them, and re-layouts, start_sector(): lax.dynamic_update_slice_in_dim(u_next, current_block, (newest ^ q) * see...  6.1 us
  transfers between devices with their start and end apart: 9, of which 6 were waited for; matrix products, arithmetic and copies ran while one was open for 3% of the time, Pallas kernels for 0%

profile of v1, /device:TPU:0, one launch (start us, length us, event | category | flops | bytes accessed | tf_op | source)
XLA Modules:
  0.0 252.7 jit_solution(12054946189291600071)
XLA Ops:
  6.5 3.0 %constant_dynamic-slice_fusion = (bf16[1,512,300]{1,2,0:T(8,128)(2,1)S(1)}, bf16[1,512,300]{1,2,0:T(8,128)(2,1)S(1)}, bf16[1,512,300]{1,2,0:T(8,128)(2,1)}, bf16...) fusion(bf16[1,512,2400]{1,2,0:T(8,128)(2,1)} %param.4, ...), kind=kLoop, calls=%fused_computation.21 | loop fusion | bytes 4300828 | tf_op jit(solution)/shard_map/dynamic_slice | solution.py:21
  10.0 2.6 %collective-permute-start.1 = (bf16[1,512,300]{1,2,0:T(8,128)(2,1)}, bf16[1,512,300]{1,2,0:T(8,128)(2,1)}, u32[]{:S(2)}, u32[]{:S(2)}) collective-permute-start(bf16[1,512,300]{1,2,0:T(8,128)(2,1)} %get-tuple-element.15), channel_id=1, source_target_pairs={{0,4},{1,5},{4,0},{5,1},{8,12},{9,13},{12,8},{13,9},{2,6},{3,7},{6... | collective-permute-start | bytes 921608 | tf_op jit(solution)/shard_map/ppermute | solution.py:23
  12.7 2.7 %collective-permute-start.3 = (bf16[1,512,300]{1,2,0:T(8,128)(2,1)}, bf16[1,512,300]{1,2,0:T(8,128)(2,1)}, u32[]{:S(2)}, u32[]{:S(2)}) collective-permute-start(bf16[1,512,300]{1,2,0:T(8,128)(2,1)} %get-tuple-element.13), channel_id=1, source_target_pairs={{0,8},{1,9},{4,12},{5,13},{8,0},{9,1},{12,4},{13,5},{2,10},{3,11},... | collective-permute-start | bytes 921608 | tf_op jit(solution)/shard_map/ppermute | solution.py:23
  15.4 0.6 fusion.10
  17.6 1.1 bitcast_dynamic-update-slice_fusion.7
  18.6 3.6 %collective-permute-start.5 = (bf16[1,512,300]{1,2,0:T(8,128)(2,1)S(1)}, bf16[1,512,300]{1,2,0:T(8,128)(2,1)S(1)}, u32[]{:S(2)}, u32[]{:S(2)}) collective-permute-start(bf16[1,512,300]{1,2,0:T(8,128)(2,1)S(1)} %get-tuple-element.17), channel_id=1, source_target_pairs={{0,12},{1,13},{4,8},{5,9},{8,4},{9,5},{12,0},{13,1},{2,14},{3,15},... | collective-permute-start | bytes 921608 | tf_op jit(solution)/shard_map/ppermute | solution.py:23
  22.2 1.0 bitcast_dynamic-update-slice_fusion.6
  23.2 10.7 %collective-permute-done.1 = bf16[1,512,300]{1,2,0:T(8,128)(2,1)} collective-permute-done((bf16[1,512,300]{1,2,0:T(8,128)(2,1)}, bf16[1,512,300]{1,2,0:T(8,128)(2,1)}, u32[]{:S(2)}, u32[]{:S(2)}) %collective-permute-start.1) | collective-permute-done | bytes 307232 | tf_op jit(solution)/shard_map/ppermute | solution.py:23
  33.9 0.7 collective-permute-start.6
  34.6 1.0 bitcast_dynamic-update-slice_fusion.5
  35.7 4.6 %collective-permute-done.2 = bf16[1,512,300]{1,2,0:T(8,128)(2,1)} collective-permute-done((bf16[1,512,300]{1,2,0:T(8,128)(2,1)}, bf16[1,512,300]{1,2,0:T(8,128)(2,1)}, u32[]{:S(2)}, u32[]{:S(2)}) %collective-permute-start.2) | collective-permute-done | bytes 307232 | tf_op jit(solution)/shard_map/ppermute | solution.py:23
  40.3 1.0 bitcast_dynamic-update-slice_fusion.4
  41.3 1.0 bitcast_dynamic-update-slice_fusion.3
  42.3 1.0 bitcast_dynamic-update-slice_fusion.2
  43.3 6.9 %collective-permute-done.5 = bf16[1,512,300]{1,2,0:T(8,128)(2,1)S(1)} collective-permute-done((bf16[1,512,300]{1,2,0:T(8,128)(2,1)S(1)}, bf16[1,512,300]{1,2,0:T(8,128)(2,1)S(1)}, u32[]{:S(2)}, u32[]{:S(2)}) %collective-permute-start.5) | collective-permute-done | bytes 307232 | tf_op jit(solution)/shard_map/ppermute | solution.py:23
  50.2 5.9 %collective-permute-done.6 = bf16[1,512,300]{1,2,0:T(8,128)(2,1)S(1)} collective-permute-done((bf16[1,512,300]{1,2,0:T(8,128)(2,1)S(1)}, bf16[1,512,300]{1,2,0:T(8,128)(2,1)S(1)}, u32[]{:S(2)}, u32[]{:S(2)}) %collective-permute-start.6) | collective-permute-done | bytes 307232 | tf_op jit(solution)/shard_map/ppermute | solution.py:23
  56.1 2.6 %broadcast_select_fusion.1 = (bf16[4096,300]{0,1:T(8,128)(2,1)}, bf16[4096,300]{0,1:T(8,128)(2,1)}) fusion(bf16[4096,300]{0,1:T(8,128)(2,1)S(1)} %bitcast_dynamic-update-slice_fusion, pred[]{:T(512)S(6)} %eq.10, pred[]{:T(512)S(6)} %eq.11), kind=kLoop, calls=%fused_computation.3 | loop fusion | flops 2457600 | bytes 7372802 | tf_op jit(solution)/shard_map/jit(_where)/select_n | solution.py:36
  59.0 125.7 %all-reduce.7.cloned.1.call-done = (bf16[4096,300]{0,1:T(8,128)(2,1)}, bf16[4096,300]{0,1:T(8,128)(2,1)}) async-done(((bf16[4096,300]{0,1:T(8,128)(2,1)}, bf16[4096,300]{0,1:T(8,128)(2,1)}), (bf16[4096,300]{0,1:T(8,128)(2,1)}, bf16[4096,300]{0,1:T(8,128)(2,1)})) %all-reduce.7.cloned.1.call-update) | async-done | bytes 4915216 | tf_op jit(solution)/shard_map/psum | solution.py:37
  184.6 4.1 %fusion.11 = f32[300,300]{1,0:T(8,128)} fusion(bf16[4096,300]{0,1:T(8,128)(2,1)S(1)} %bitcast_dynamic-update-slice_fusion, bf16[4096,300]{0,1:T(8,128)(2,1)} %get-tuple-element.8), kind=kOutput, calls=%fused_computation.34 | convolution fusion | flops 737280000 | bytes 5275200 | tf_op jit(solution)/shard_map/dot_general | solution.py:59
  188.7 2.2 fusion.12
  193.0 35.9 %all-reduce.5.cloned.1.call-done = (f32[300,300]{1,0:T(8,128)}, f32[300,300]{1,0:T(8,128)}) async-done(((f32[300,300]{1,0:T(8,128)}, f32[300,300]{1,0:T(8,128)}), (f32[300,300]{1,0:T(8,128)}, f32[300,300]{1,0:T(8,128)})) %all-reduce.5.cloned.1.call-update) | async-done | bytes 720016 | tf_op jit(solution)/shard_map/psum | solution.py:62
  228.9 3.4 %fusion.1 = f32[4096,300]{0,1:T(8,128)S(1)} fusion(bf16[4096,300]{0,1:T(8,128)(2,1)} %get-tuple-element.7, f32[300,300]{1,0:T(8,128)} %get-tuple-element.5, f32[300]{0:T(512)S(1)} %get-tuple-element.20, f32[300]{0:T(512)S(1)} %get-tuple-element.19), kind=kOutput, calls=%fused_computation.14 | convolution fusion | flops 737640000 | bytes 7735200 | tf_op jit(solution)/shard_map/dot_general | solution.py:64
  232.4 3.8 %fusion = f32[1,4096,300]{1,2,0:T(8,128)} fusion(f32[4096,300]{0,1:T(8,128)S(1)} %fusion.1, bf16[4096,300]{0,1:T(8,128)(2,1)S(1)} %copy-done, f32[300,300]{1,0:T(8,128)S(1)} %copy-done.2, f32[300]{0:T(512)S(1)} %get-tuple-element.18, f32[300]{0:T(512)S(1)} %get-tuple-element.19), kind=kOutput, calls=%fused_computation.1 | convolution fusion | flops 738868800 | bytes 12650400 | tf_op jit(solution)/shard_map/dot_general | solution.py:64
  236.2 9.7 %copy.5 = f32[1,4096,300]{1,0,2:T(1,128)} copy(f32[1,4096,300]{1,2,0:T(8,128)} %fusion) | data formatting | bytes 9830400 | tf_op jit(solution)/shard_map/broadcast_in_dim | solution.py:67
  (24 shorter events, 1.3 us)
Async XLA Ops:
  6.5 8.9 %copy-start.4 = (s32[2]{0:T(128)S(1)}, s32[2]{0:T(128)}, u32[]{:S(2)}) copy-start(s32[2]{0:T(128)} %param.7) | copy-start | bytes 28
  6.5 178.1 %all-reduce.7.cloned.1.call-start = ((), (), s32[]{:S(2)}) async-start(), calls=%async_computation.1 | async-start | bytes 9961472 | tf_op jit(solution)/shard_map/psum | solution.py:37
  9.5 9.1 %collective-permute-start = (bf16[1,512,300]{1,2,0:T(8,128)(2,1)}, bf16[1,512,300]{1,2,0:T(8,128)(2,1)}, u32[]{:S(2)}, u32[]{:S(2)}) collective-permute-start(bf16[1,512,300]{1,2,0:T(8,128)(2,1)} %get-tuple-element.16), channel_id=1, source_target_pairs={{0,1},{1,0},{4,5},{5,4},{8,9},{9,8},{12,13},{13,12},{2,3},{3,2},{6... | collective-permute-start | bytes 921608 | tf_op jit(solution)/shard_map/ppermute | solution.py:23
  10.0 24.0 %collective-permute-start.1 = (bf16[1,512,300]{1,2,0:T(8,128)(2,1)}, bf16[1,512,300]{1,2,0:T(8,128)(2,1)}, u32[]{:S(2)}, u32[]{:S(2)}) collective-permute-start(bf16[1,512,300]{1,2,0:T(8,128)(2,1)} %get-tuple-element.15), channel_id=1, source_target_pairs={{0,4},{1,5},{4,0},{5,1},{8,12},{9,13},{12,8},{13,9},{2,6},{3,7},{6... | collective-permute-start | bytes 921608 | tf_op jit(solution)/shard_map/ppermute | solution.py:23
  12.6 27.7 %collective-permute-start.2 = (bf16[1,512,300]{1,2,0:T(8,128)(2,1)}, bf16[1,512,300]{1,2,0:T(8,128)(2,1)}, u32[]{:S(2)}, u32[]{:S(2)}) collective-permute-start(bf16[1,512,300]{1,2,0:T(8,128)(2,1)} %get-tuple-element.14), channel_id=1, source_target_pairs={{0,5},{1,4},{4,1},{5,0},{8,13},{9,12},{12,9},{13,8},{2,7},{3,6},{6... | collective-permute-start | bytes 921608 | tf_op jit(solution)/shard_map/ppermute | solution.py:23
  12.7 28.6 %collective-permute-start.3 = (bf16[1,512,300]{1,2,0:T(8,128)(2,1)}, bf16[1,512,300]{1,2,0:T(8,128)(2,1)}, u32[]{:S(2)}, u32[]{:S(2)}) collective-permute-start(bf16[1,512,300]{1,2,0:T(8,128)(2,1)} %get-tuple-element.13), channel_id=1, source_target_pairs={{0,8},{1,9},{4,12},{5,13},{8,0},{9,1},{12,4},{13,5},{2,10},{3,11},... | collective-permute-start | bytes 921608 | tf_op jit(solution)/shard_map/ppermute | solution.py:23
  15.4 26.9 %collective-permute-start.4 = (bf16[1,512,300]{1,2,0:T(8,128)(2,1)S(1)}, bf16[1,512,300]{1,2,0:T(8,128)(2,1)}, u32[]{:S(2)}, u32[]{:S(2)}) collective-permute-start(bf16[1,512,300]{1,2,0:T(8,128)(2,1)S(1)} %get-tuple-element.12), channel_id=1, source_target_pairs={{0,9},{1,8},{4,13},{5,12},{8,1},{9,0},{12,5},{13,4},{2,11},{3,10},... | collective-permute-start | bytes 921608 | tf_op jit(solution)/shard_map/ppermute | solution.py:23
  18.6 31.5 %collective-permute-start.5 = (bf16[1,512,300]{1,2,0:T(8,128)(2,1)S(1)}, bf16[1,512,300]{1,2,0:T(8,128)(2,1)S(1)}, u32[]{:S(2)}, u32[]{:S(2)}) collective-permute-start(bf16[1,512,300]{1,2,0:T(8,128)(2,1)S(1)} %get-tuple-element.17), channel_id=1, source_target_pairs={{0,12},{1,13},{4,8},{5,9},{8,4},{9,5},{12,0},{13,1},{2,14},{3,15},... | collective-permute-start | bytes 921608 | tf_op jit(solution)/shard_map/ppermute | solution.py:23
  33.9 22.1 %collective-permute-start.6 = (bf16[1,512,300]{1,2,0:T(8,128)(2,1)S(1)}, bf16[1,512,300]{1,2,0:T(8,128)(2,1)S(1)}, u32[]{:S(2)}, u32[]{:S(2)}) collective-permute-start(bf16[1,512,300]{1,2,0:T(8,128)(2,1)S(1)} %get-tuple-element.11), channel_id=1, source_target_pairs={{0,13},{1,12},{4,9},{5,8},{8,5},{9,4},{12,1},{13,0},{2,15},{3,14},... | collective-permute-start | bytes 921608 | tf_op jit(solution)/shard_map/ppermute | solution.py:23
  58.7 170.2 %all-reduce.5.cloned.1.call-start = ((), (), s32[]{:S(2)}) async-start(), calls=%async_computation | async-start | bytes 1867776 | tf_op jit(solution)/shard_map/psum | solution.py:62
  184.6 4.1 %copy-start.1 = (bf16[4096,300]{0,1:T(8,128)(2,1)S(1)}, bf16[4096,300]{0,1:T(8,128)(2,1)}, u32[]{:S(2)}) copy-start(bf16[4096,300]{0,1:T(8,128)(2,1)} %get-tuple-element.7) | copy-start | bytes 7372804
  188.7 4.1 %copy-start.3 = (f32[2400]{0:T(1024)S(1)}, f32[2400]{0:T(1024)}, u32[]{:S(2)}) copy-start(f32[2400]{0:T(1024)} %param.6) | copy-start | bytes 28804
  228.9 3.4 %copy-start = (bf16[4096,300]{0,1:T(8,128)(2,1)S(1)}, bf16[4096,300]{0,1:T(8,128)(2,1)}, u32[]{:S(2)}) copy-start(bf16[4096,300]{0,1:T(8,128)(2,1)} %get-tuple-element.8) | copy-start | bytes 7372804
  228.9 3.4 %copy-start.2 = (f32[300,300]{1,0:T(8,128)S(1)}, f32[300,300]{1,0:T(8,128)}, u32[]{:S(2)}) copy-start(f32[300,300]{1,0:T(8,128)} %get-tuple-element.6) | copy-start | bytes 1080004
Sparse Core Ops, SparseCore 0:
  58.9 125.7 all-reduce.6
  191.1 37.7 all-reduce.4
